TPU v7x, 256 devices: a whole 4x4x8 slice. The times are simulated.
256 devices in a mesh: dp: 64 (over y, z, core), seq: 4 (over x).
Axes of the slice: x: 4, y: 4, z: 8, core: 2. Of those that a mesh axis runs over, the one named last changes fastest.
Arguments:
- frames: bfloat16 [32768, 1536], P('dp', 'seq')
- owner_slot: int32 [32768], P('dp'), may hold values from -1 to 32767, as said below
- segment: int32 [64, 512], P('dp'), may hold values from 0 to 2, never falling along the last dimension, each value on 1 to 256 neighbouring positions
- norm_gain: float32 [1536], replicated, may hold values from 0.25 to 1.75
- expand: bfloat16 [1536, 2, 1536], P('dp', None, 'seq'), may hold values from -0.15625 to 0.15625
- kernel: float32 [9, 1536], P(None, 'seq'), may hold values from -2.5 to 2.5
- project: bfloat16 [1536, 1536], P('seq', 'dp'), may hold values from -0.15625 to 0.15625
- cotangent: bfloat16 [32768, 1536], P('dp', 'seq'), may hold values from -6 to 6
Outputs:
- output: bfloat16 [32768, 1536], P('dp', 'seq')
- grad_frames: bfloat16 [32768, 1536], P('dp', 'seq')
- grad_gain: float32 [1536], P('seq')
- grad_kernel: float32 [9, 1536], P(None, 'seq')
- grad_expand: float32 [1536, 2, 1536], P('dp', None, 'seq')
- grad_project: float32 [1536, 1536], P('seq', 'dp')
Inputs may be any that keep to these rules, and one draw needn't show every extreme that they name: `owner_slot`: for each arrival row, the balanced row that takes it, or -1 for an empty arrival row; no balanced row is named twice. The live rows of each pack come first, contiguous, ordered by sending index of dp and then by arrival row; empty rows fill the pack's tail. Of the 512 arrival rows of one index of dp, at most 8 name rows of any one pack; some pack takes exactly 8 rows from every index of dp. `segment`: within each pack the utterance numbers never fall; a pack holds 3 utterances of 1 to 256 frames, one of exactly 256.
All inputs are finite; a program needn't handle non-finite values.
Results may differ from a plain program's by a relative error of at most 0.01.
Values may be sent and summed in bfloat16 or wider, within the bound.
No kernel may reach another device: no remote copies, remote signals or barrier semaphores. Data moves between devices by JAX's collectives and lax.ppermute only.
A program may use at most 128 MiB of HBM per device.

v0:
```python
import math
import jax
import jax.numpy as jnp
from jax import lax
from jax.sharding import PartitionSpec as P

D = 1536
KSIZE = 9
EPS = 1e-05


def conv_masks(labels):
    half_width = (KSIZE - 1) // 2
    length = labels.shape[0]
    padded = jnp.pad(labels, (half_width, half_width), constant_values=-1)
    return [
        (padded[tap_index : tap_index + length] == labels).astype(jnp.float32)[:, None]
        for tap_index in range(KSIZE)
    ]


def depthwise(signal, kernel, tap_masks):
    half_width = (KSIZE - 1) // 2
    length = signal.shape[0]
    padded = jnp.pad(signal, ((half_width, half_width), (0, 0)))
    total = jnp.zeros(signal.shape, jnp.float32)
    for tap_index in range(KSIZE):
        total = (
            total
            + kernel[tap_index] * padded[tap_index : tap_index + length] * tap_masks[tap_index]
        )
    return total


def depthwise_back(signal, upstream, kernel, tap_masks):
    half_width = (KSIZE - 1) // 2
    length = signal.shape[0]
    padded = jnp.pad(signal, ((half_width, half_width), (0, 0)))
    spread = jnp.zeros((length + 2 * half_width, signal.shape[1]), jnp.float32)
    tap_sums = []
    for tap_index in range(KSIZE):
        masked = upstream * tap_masks[tap_index]
        tap_sums.append(jnp.sum(masked * padded[tap_index : tap_index + length], axis=0))
        spread = spread + jnp.pad(
            kernel[tap_index] * masked, ((tap_index, 2 * half_width - tap_index), (0, 0))
        )
    return (jnp.stack(tap_sums), spread[half_width : half_width + length])


def place_rows(incoming, landing, row_count):
    flat = incoming.reshape(-1, incoming.shape[-1])
    total_slots = flat.shape[0]
    inverse = (
        jnp.full((row_count + 1,), total_slots, jnp.int32)
        .at[landing.reshape(-1)]
        .set(jnp.arange(total_slots, dtype=jnp.int32))[:row_count]
    )
    padded = jnp.concatenate([flat, jnp.zeros((1, flat.shape[1]), flat.dtype)])
    return (padded[inverse], inverse < total_slots)


def shards(frames, owner_slot, segment, norm_gain, expand, kernel, project, cotangent):
    row_count, quarter = frames.shape
    groups = lax.axis_size("dp")
    lane_index = lax.axis_index("seq")
    capacity = row_count // groups
    bucket_slots = groups * capacity
    dest_group = jnp.where(owner_slot >= 0, owner_slot // row_count, groups)
    onehot = (dest_group[:, None] == jnp.arange(groups, dtype=jnp.int32)[None, :]).astype(jnp.int32)
    earlier = jnp.cumsum(onehot, axis=0) - onehot
    within = jnp.sum(earlier * onehot, axis=1)
    send_pos = jnp.where(owner_slot >= 0, dest_group * capacity + within, bucket_slots)
    source_row = (
        jnp.full((bucket_slots + 1,), row_count, jnp.int32)
        .at[send_pos]
        .set(jnp.arange(row_count, dtype=jnp.int32))[:bucket_slots]
    )
    slot_padded = jnp.concatenate([owner_slot, jnp.full((1,), -1, jnp.int32)])
    named_slot = slot_padded[source_row]
    landing_out = jnp.where(named_slot >= 0, named_slot % row_count, row_count).reshape(
        groups, capacity
    )
    padded_in = jnp.concatenate([frames, jnp.zeros((1, quarter), jnp.bfloat16)])
    outgoing = padded_in[source_row].reshape(groups, capacity, quarter)
    incoming, landing = (
        lax.all_to_all(outgoing, "dp", split_axis=0, concat_axis=0, tiled=True),
        lax.all_to_all(landing_out, "dp", split_axis=0, concat_axis=0, tiled=True),
    )
    local_rows, occupied = place_rows(incoming, landing, row_count)
    whole_rows = lax.all_gather(local_rows, "seq", axis=1, tiled=True)
    live_col = occupied.astype(jnp.float32)[:, None]
    floats = whole_rows.astype(jnp.float32)
    row_mean = jnp.mean(floats, axis=1, keepdims=True)
    centred = floats - row_mean
    inv_scale = lax.rsqrt(jnp.mean(centred * centred, axis=1, keepdims=True) + EPS)
    normed = centred * inv_scale
    scaled = (normed * norm_gain).astype(jnp.bfloat16)
    expand_full = lax.all_gather(expand, "dp", axis=0, tiled=True).reshape(D, 2 * quarter)
    project_full = lax.all_gather(project, "dp", axis=1, tiled=True)
    joined = jnp.dot(scaled, expand_full, preferred_element_type=jnp.float32)
    value_half = joined[:, :quarter]
    gate_sig = jax.nn.sigmoid(joined[:, quarter:])
    glu_out = value_half * gate_sig
    tap_masks = conv_masks(segment[0])
    conv_out = depthwise(glu_out, kernel, tap_masks)
    conv_sig = jax.nn.sigmoid(conv_out)
    hidden = (conv_out * conv_sig * live_col).astype(jnp.bfloat16)
    partial_out = jnp.dot(hidden, project_full, preferred_element_type=jnp.float32)
    mixed_share = lax.psum_scatter(
        partial_out.astype(jnp.bfloat16), "seq", scatter_dimension=1, tiled=True
    ).astype(jnp.float32)
    output = (local_rows.astype(jnp.float32) + mixed_share).astype(jnp.bfloat16)
    inv_root = 1.0 / math.sqrt(row_count * groups)
    cot_full = lax.all_gather(cotangent, "seq", axis=1, tiled=True)
    project_term = lax.dot_general(
        hidden, cot_full, (((0,), (0,)), ((), ())), preferred_element_type=jnp.float32
    )
    grad_project = lax.psum_scatter(project_term, "dp", scatter_dimension=1, tiled=True) * inv_root
    hidden_grad = (
        lax.dot_general(
            cot_full, project_full, (((1,), (1,)), ((), ())), preferred_element_type=jnp.float32
        )
        * live_col
    )
    conv_grad = hidden_grad * (conv_sig + conv_out * conv_sig * (1.0 - conv_sig))
    kernel_term, glu_grad = depthwise_back(glu_out, conv_grad, kernel, tap_masks)
    proj_grad = jnp.concatenate(
        [glu_grad * gate_sig, glu_grad * value_half * gate_sig * (1.0 - gate_sig)], axis=1
    ).astype(jnp.bfloat16)
    term_block = lax.dot_general(
        scaled, proj_grad, (((0,), (0,)), ((), ())), preferred_element_type=jnp.float32
    )
    grad_expand = (
        lax.psum_scatter(
            term_block.reshape(expand.shape[0] * lax.axis_size("dp"), 2, quarter),
            "dp",
            scatter_dimension=0,
            tiled=True,
        )
        * inv_root
    )
    scaled_part = lax.dot_general(
        proj_grad, expand_full, (((1,), (1,)), ((), ())), preferred_element_type=jnp.float32
    )
    normed_local = lax.dynamic_slice_in_dim(normed, lane_index * quarter, quarter, 1)
    scaled_grad = lax.psum(scaled_part.astype(jnp.bfloat16), "seq").astype(jnp.float32)
    normed_grad = scaled_grad * norm_gain
    first_mean = jnp.mean(normed_grad, axis=1, keepdims=True)
    second_mean = jnp.mean(normed_grad * normed, axis=1, keepdims=True)
    full_grad = inv_scale * (normed_grad - first_mean - normed * second_mean)
    packed_grad = lax.dynamic_slice_in_dim(full_grad, lane_index * quarter, quarter, 1)
    scaled_share = lax.dynamic_slice_in_dim(scaled_grad, lane_index * quarter, quarter, 1)
    gain_term = jnp.sum(scaled_share * normed_local, axis=0)
    gain_sum, kernel_sum = lax.psum((gain_term, kernel_term), "dp")
    back_rows = (packed_grad + cotangent.astype(jnp.float32)).astype(jnp.bfloat16)
    back_padded = jnp.concatenate([back_rows, jnp.zeros((1, quarter), jnp.bfloat16)])
    returning = back_padded[landing.reshape(-1)].reshape(groups, capacity, quarter)
    returned = lax.all_to_all(returning, "dp", split_axis=0, concat_axis=0, tiled=True)
    returned_flat = jnp.concatenate(
        [returned.reshape(bucket_slots, quarter), jnp.zeros((1, quarter), jnp.bfloat16)]
    )
    grad_frames = returned_flat[send_pos]
    return (
        output,
        grad_frames,
        gain_sum * inv_root,
        kernel_sum * inv_root,
        grad_expand,
        grad_project,
    )


def solution(mesh):
    placed = (
        P("dp", "seq"),
        P("dp"),
        P("dp", None),
        P(),
        P("dp", None, "seq"),
        P(None, "seq"),
        P("seq", "dp"),
        P("dp", "seq"),
    )
    return jax.shard_map(
        shards,
        mesh=mesh,
        in_specs=placed,
        out_specs=(
            P("dp", "seq"),
            P("dp", "seq"),
            P("seq"),
            P(None, "seq"),
            P("dp", None, "seq"),
            P("seq", "dp"),
        ),
        check_vma=False,
    )
```

profile of v0, /device:TPU:4, one launch (start us, length us, event | category | flops | bytes accessed | tf_op | source)
XLA Modules:
  0.0 722.8 jit_solution(6718990988851698500)
XLA Ops:
  7.2 0.7 fusion.22
  7.9 0.7 fusion.55
  8.6 1.2 reduce-window.6
  10.2 0.7 compare_select_fusion.3
  10.9 2.4 scatter_custom_fusion
  13.4 0.7 pad_add_fusion.7
  14.1 2.3 gather_fusion.1
  17.1 12.1 %all-to-all-start.1 = ((s32[64,1,8]{2,1,0:T(1,128)}), s32[64,1,8]{2,1,0:T(1,128)S(1)}, u32[]{:S(2)}, u32[]{:S(2)}) async-start(s32[64,1,8]{2,1,0:T(1,128)} %bitcast.4), calls=%async_computation.1 | async-start | bytes 65536 | tf_op jit(solution)/shard_map/all_to_all | solution.py:87
  29.3 2.6 gather_fusion
  31.9 6.8 all-to-all-done.1
  38.7 4.6 all-to-all-start
  43.9 0.7 reduce.23
  44.8 2.4 scatter_custom_fusion.1
  47.2 10.6 %all-to-all-done = bf16[64,8,384]{2,1,0:T(8,128)(2,1)S(1)} async-done(((bf16[64,8,384]{2,1,0:T(8,128)(2,1)}), bf16[64,8,384]{2,1,0:T(8,128)(2,1)S(1)}, u32[]{:S(2)}, u32[]{:S(2)}) %all-to-all-start) | async-done | bytes 393248 | tf_op jit(solution)/shard_map/all_to_all | solution.py:86
  57.9 2.6 gather_fusion.2
  60.6 0.7 all-gather.6.cloned.1.call-update
  61.3 0.7 all-gather.8.cloned.1.call-update
  63.0 22.6 %all-gather.12.cloned.1.call-done = bf16[512,1536]{1,0:T(8,128)(2,1)} async-done(((bf16[512,384]{1,0:T(8,128)(2,1)}), bf16[512,1536]{1,0:T(8,128)(2,1)}) %all-gather.12.cloned.1.call-update) | async-done | bytes 1572880 | tf_op jit(solution)/shard_map/all_gather | solution.py:90
  85.6 1.8 convert_reduce_fusion
  88.0 79.3 %all-gather.6.cloned.1.call-done = bf16[1536,2,384]{2,1,0:T(2,128)(2,1)} async-done(((bf16[24,2,384]{2,1,0:T(2,128)(2,1)}), bf16[1536,2,384]{2,1,0:T(2,128)(2,1)}) %all-gather.6.cloned.1.call-update) | async-done | bytes 2359312 | tf_op jit(solution)/shard_map/all_gather | solution.py:98
  167.3 2.1 copy.23
  169.5 1.5 fusion.13
  171.2 0.9 copy-done.3
  172.1 2.0 multiply_add_fusion
  174.1 70.2 %all-gather.8.cloned.1.call-done = bf16[384,1536]{0,1:T(8,128)(2,1)} async-done(((bf16[384,24]{0,1:T(8,128)(2,1)}), bf16[384,1536]{0,1:T(8,128)(2,1)}) %all-gather.8.cloned.1.call-update) | async-done | bytes 1179664 | tf_op jit(solution)/shard_map/all_gather | solution.py:99
  244.4 27.2 %all-gather.10.cloned.1.call-done = bf16[512,1536]{1,0:T(8,128)(2,1)} async-done(((bf16[512,384]{1,0:T(8,128)(2,1)}), bf16[512,1536]{1,0:T(8,128)(2,1)}) %all-gather.10.cloned.1.call-update) | async-done | bytes 1572880 | tf_op jit(solution)/shard_map/all_gather | solution.py:114
  271.6 7.9 %multiply_reduce_fusion.1 = (f32[384]{0:T(512)}, f32[384]{0:T(512)}, f32[384]{0:T(512)}, f32[384]{0:T(512)}, f32[384]{0:T(512)}, /*index=5*/f32[384]{0:T(512)}, ...) fusion(f32[512,384]{1,0:T(8,128)} %copy-done.3, ...), kind=kOutput, calls=%fused_computation.36 | convolution fusion | flops 611054208 | bytes 5932032 | tf_op jit(solution)/shard_map/dot_general | solution.py:120
  279.5 0.7 multiply_multiply_fusion.7
  281.3 0.7 copy-done.8
  282.0 0.8 copy-done.5
  282.8 2.6 convolution_convert_fusion
  285.5 4.8 fusion.12
  290.3 8.2 %copy.19 = f32[1536,2,384]{2,1,0:T(2,128)} copy(f32[1536,2,384]{0,2,1:T(8,128)} %bitcast.41) | data formatting | bytes 9437184 | tf_op jit(solution)/shard_map/reshape | solution.py:135
  299.1 2.6 convolution_convert_fusion.1
  301.7 1.6 copy.20
  303.5 4.2 fusion.46
  308.4 32.9 %all-reduce.21.cloned.1.call-done = bf16[512,1536]{1,0:T(8,128)(2,1)} async-done(((bf16[512,1536]{1,0:T(8,128)(2,1)}), bf16[512,1536]{1,0:T(8,128)(2,1)}) %all-reduce.21.cloned.1.call-update) | async-done | bytes 1572880 | tf_op jit(solution)/shard_map/psum | solution.py:146
  341.3 1.9 convert_element_type.110
  343.2 1.1 fusion.11
  344.8 2.6 gather_fusion.3
  347.4 10.5 %all-to-all-start.2 = ((bf16[64,8,384]{2,1,0:T(8,128)(2,1)}), bf16[64,8,384]{2,1,0:T(8,128)(2,1)S(1)}, u32[]{:S(2)}, u32[]{:S(2)}) async-start(bf16[64,8,384]{2,1,0:T(8,128)(2,1)} %bitcast.7), calls=%async_computation.2 | async-start | bytes 786432 | tf_op jit(solution)/shard_map/all_to_all | solution.py:158
  359.4 251.8 %all-reduce.17 = (f32[384]{0:T(512)S(1)}, f32[9,384]{1,0:T(8,128)S(1)}) all-reduce(f32[384]{0:T(512)S(1)} %get-tuple-element.30, f32[9,384]{1,0:T(8,128)S(1)} %stack.39), channel_id=1, replica_groups=mesh['dp'=64,'seq'=4] {'dp'}, use_global_device_ids=true, to_apply=%region_12.13 | all-reduce | flops 3840 | bytes 30720 | tf_op jit(solution)/shard_map/psum | solution.py:154
  612.4 2.6 gather_fusion.4
  615.0 1.6 dynamic-slice_multiply_fusion
  616.6 1.2 copy.21
  617.8 0.8 add_convert_fusion
  618.6 95.9 %reduce-scatter.9.cloned.1.call-done = f32[384,24]{0,1:T(8,128)} async-done(((f32[384,1536]{0,1:T(8,128)}), f32[384,24]{0,1:T(8,128)}) %reduce-scatter.9.cloned.1.call-update) | async-done | bytes 36880
  714.6 1.4 broadcast_multiply_fusion.2
  (117 shorter events, 8.9 us)
Async XLA Ops:
  7.2 22.1 %copy-start.7 = (bf16[512,384]{1,0:T(8,128)(2,1)S(1)}, bf16[512,384]{1,0:T(8,128)(2,1)}, u32[]{:S(2)}) copy-start(bf16[512,384]{1,0:T(8,128)(2,1)} %param.8) | copy-start | bytes 1179652
  10.9 3.2 copy-start.10
  17.1 21.6 %all-to-all-start.1 = ((s32[64,1,8]{2,1,0:T(1,128)}), s32[64,1,8]{2,1,0:T(1,128)S(1)}, u32[]{:S(2)}, u32[]{:S(2)}) async-start(s32[64,1,8]{2,1,0:T(1,128)} %bitcast.4), calls=%async_computation.1 | async-start | bytes 65536 | tf_op jit(solution)/shard_map/all_to_all | solution.py:87
  38.7 19.1 %all-to-all-start = ((bf16[64,8,384]{2,1,0:T(8,128)(2,1)}), bf16[64,8,384]{2,1,0:T(8,128)(2,1)S(1)}, u32[]{:S(2)}, u32[]{:S(2)}) async-start(bf16[64,8,384]{2,1,0:T(8,128)(2,1)} %bitcast.2), calls=%async_computation | async-start | bytes 786432 | tf_op jit(solution)/shard_map/all_to_all | solution.py:86
  43.3 42.2 %all-gather.12.cloned.1.call-start = ((), (), s32[]{:S(2)}) async-start(), calls=%async_computation.9 | async-start | bytes 1966080 | tf_op jit(solution)/shard_map/all_gather | solution.py:90
  44.7 13.1 %copy-start.12 = (s32[512,1]{0,1:T(1,128)}, s32[512,1]{0,1:T(1,128)S(1)}, u32[]{:S(2)}) copy-start(s32[512,1]{0,1:T(1,128)S(1)} %compare_select_fusion) | copy-start | bytes 6148
  57.9 4.9 copy-start.14
  57.9 5.0 copy-start.15
  60.5 106.8 %all-gather.6.cloned.1.call-start = ((), (), s32[]{:S(2)}) async-start(), calls=%async_computation.5 | async-start | bytes 2396160 | tf_op jit(solution)/shard_map/all_gather | solution.py:98
  61.3 183.1 %all-gather.8.cloned.1.call-start = ((), (), s32[]{:S(2)}) async-start(), calls=%async_computation.6 | async-start | bytes 1198080 | tf_op jit(solution)/shard_map/all_gather | solution.py:99
  62.0 209.6 %all-gather.10.cloned.1.call-start = ((), (), s32[]{:S(2)}) async-start(), calls=%async_computation.7 | async-start | bytes 1966080 | tf_op jit(solution)/shard_map/all_gather | solution.py:114
  62.6 278.7 %all-reduce.21.cloned.1.call-start = ((), (), s32[]{:S(2)}) async-start(), calls=%async_computation.8 | async-start | bytes 3145728 | tf_op jit(solution)/shard_map/psum | solution.py:146
  63.0 208.7 %copy-start.25 = (f32[512]{0:T(512)}, f32[512]{0:T(512)S(1)}, u32[]{:S(2)}) copy-start(f32[512]{0:T(512)S(1)} %compare_convert_fusion) | copy-start | bytes 6148
  85.6 1.9 copy-start
  167.3 2.2 copy-start.9
  169.5 1.5 copy-start.4
  171.2 0.9 copy-start.3
  281.0 1.8 copy-start.5
  281.3 0.7 copy-start.8
  285.5 329.6 %all-reduce.23.cloned.1.call-start = ((), (), s32[]{:S(2)}) async-start(), calls=%async_computation.11 | async-start | bytes 9437184
  298.4 0.7 copy-start.26
  298.4 318.1 %reduce-scatter.7.cloned.1.call-start = ((), (), s32[]{:S(2)}) async-start(), calls=%async_computation.10 | async-start | bytes 1966080
  303.3 411.3 %reduce-scatter.9.cloned.1.call-start = ((), (), s32[]{:S(2)}) async-start(), calls=%async_computation.12 | async-start | bytes 2396160
  307.7 0.7 copy-start.13
  341.3 1.9 copy-start.1
  343.2 1.1 copy-start.6
  344.7 13.2 %copy-start.27 = (u32[256]{0:T(256)S(1)}, u32[256]{0:T(256)}, u32[]{:S(2)}) copy-start(u32[256]{0:T(256)} %constant.110) | copy-start | bytes 3076
  344.7 14.4 %copy-start.11 = (s32[512]{0:T(512)S(1)}, s32[512]{0:T(512)}, u32[]{:S(2)}) copy-start(s32[512]{0:T(512)} %copy-done.10) | copy-start | bytes 6148
  344.7 14.4 %copy-start.24 = (f32[384]{0:T(512)S(1)}, f32[384]{0:T(512)}, u32[]{:S(2)}) copy-start(f32[384]{0:T(512)} %get-tuple-element.9) | copy-start | bytes 4612
  344.8 14.4 %copy-start.23 = (f32[384]{0:T(512)S(1)}, f32[384]{0:T(512)}, u32[]{:S(2)}) copy-start(f32[384]{0:T(512)} %get-tuple-element.10) | copy-start | bytes 4612
  344.8 14.4 %copy-start.22 = (f32[384]{0:T(512)S(1)}, f32[384]{0:T(512)}, u32[]{:S(2)}) copy-start(f32[384]{0:T(512)} %get-tuple-element.11) | copy-start | bytes 4612
  344.8 14.5 %copy-start.21 = (f32[384]{0:T(512)S(1)}, f32[384]{0:T(512)}, u32[]{:S(2)}) copy-start(f32[384]{0:T(512)} %get-tuple-element.12) | copy-start | bytes 4612
  344.8 14.5 %copy-start.20 = (f32[384]{0:T(512)S(1)}, f32[384]{0:T(512)}, u32[]{:S(2)}) copy-start(f32[384]{0:T(512)} %get-tuple-element.16) | copy-start | bytes 4612
  344.8 14.5 %copy-start.19 = (f32[384]{0:T(512)S(1)}, f32[384]{0:T(512)}, u32[]{:S(2)}) copy-start(f32[384]{0:T(512)} %get-tuple-element.13) | copy-start | bytes 4612
  344.8 14.5 %copy-start.18 = (f32[384]{0:T(512)S(1)}, f32[384]{0:T(512)}, u32[]{:S(2)}) copy-start(f32[384]{0:T(512)} %get-tuple-element.14) | copy-start | bytes 4612
  344.8 14.5 %copy-start.17 = (f32[384]{0:T(512)S(1)}, f32[384]{0:T(512)}, u32[]{:S(2)}) copy-start(f32[384]{0:T(512)} %get-tuple-element.15) | copy-start | bytes 4612
  344.8 14.5 %copy-start.16 = (f32[384]{0:T(512)S(1)}, f32[384]{0:T(512)}, u32[]{:S(2)}) copy-start(f32[384]{0:T(512)} %get-tuple-element.8) | copy-start | bytes 4612
  347.4 265.0 %all-to-all-start.2 = ((bf16[64,8,384]{2,1,0:T(8,128)(2,1)}), bf16[64,8,384]{2,1,0:T(8,128)(2,1)S(1)}, u32[]{:S(2)}, u32[]{:S(2)}) async-start(bf16[64,8,384]{2,1,0:T(8,128)(2,1)} %bitcast.7), calls=%async_computation.2 | async-start | bytes 786432 | tf_op jit(solution)/shard_map/all_to_all | solution.py:158
  612.4 5.4 copy-start.2
Sparse Core Ops, SparseCore 0:
  60.6 24.8 all-gather.11
  88.2 79.0 all-gather.5
  170.0 74.3 all-gather.7
  246.1 25.4 all-gather.9
  285.6 55.6 all-reduce.20
  344.7 201.8 all-reduce.22
  549.1 25.4 reduce-scatter.6
  578.7 135.7 reduce-scatter.8
where the time goes:
time: 724 us; the launch traced here: 723 us
  waiting for transfers between devices  348 us (48%)
  blocking collectives  252 us (35%)
  local copies, waits for them, and re-layouts  36.2 us (5%)
  starting transfers between devices  27.9 us (4%)
  matrix products  23.5 us (3%)
  other arithmetic  20.3 us (3%)
  between operations  15.4 us (2%)
    psum x1, blocking collectives, shards(): gain_sum, kernel_sum = lax.psum((gain_term, kernel_term), 'dp')  252 us
    unnamed x11, waiting for transfers between devices  97.9 us
    all_gather x1, waiting for transfers between devices, shards(): lax.all_gather(expand, 'dp', axis=0, tiled=True).reshape(D, 2 * quarter)  79.3 us
    all_gather x1, waiting for transfers between devices, shards(): project_full = lax.all_gather(project, 'dp', axis=1, tiled=True)  70.2 us
    psum x1, waiting for transfers between devices, shards(): lax.psum(scaled_part.astype(jnp.bfloat16), 'seq').astype(jnp.float32)  32.9 us
    all_gather x1, waiting for transfers between devices, shards(): cot_full = lax.all_gather(cotangent, 'seq', axis=1, tiled=True)  27.2 us
    all_gather x1, waiting for transfers between devices, shards(): whole_rows = lax.all_gather(local_rows, 'seq', axis=1, tiled=True)  22.6 us
  transfers between devices with their start and end apart: 11, of which 8 were waited for; matrix products, arithmetic and copies ran while one was open for 7% of the time, Pallas kernels for 0%

commit v1 on v0

--- a/solution.py
+++ b/solution.py
@@ -7,6 +7,27 @@
 D = 1536
 KSIZE = 9
 EPS = 1e-05
+
+
+def gather_around(array, axis, dim):
+    length, index, width = (lax.axis_size(axis), lax.axis_index(axis), array.shape[dim])
+    upward = [(i, (i + 1) % length) for i in range(length)]
+    left = [(i, (i - 1) % length) for i in range(length)]
+    out = jnp.zeros((*array.shape[:dim], length * width, *array.shape[dim + 1 :]), array.dtype)
+    out = lax.dynamic_update_slice_in_dim(out, array, index * width, axis=dim)
+    from_left = from_right = array
+    middle = length // 2
+    for turn in range(1, middle + 1):
+        from_left = lax.ppermute(from_left, axis, upward)
+        out = lax.dynamic_update_slice_in_dim(
+            out, from_left, (index - turn) % length * width, axis=dim
+        )
+        if turn < length - middle:
+            from_right = lax.ppermute(from_right, axis, left)
+            out = lax.dynamic_update_slice_in_dim(
+                out, from_right, (index + turn) % length * width, axis=dim
+            )
+    return out
 
 
 def conv_masks(labels):
@@ -111,7 +132,7 @@
     ).astype(jnp.float32)
     output = (local_rows.astype(jnp.float32) + mixed_share).astype(jnp.bfloat16)
     inv_root = 1.0 / math.sqrt(row_count * groups)
-    cot_full = lax.all_gather(cotangent, "seq", axis=1, tiled=True)
+    cot_full = gather_around(cotangent, "seq", 1)
     project_term = lax.dot_general(
         hidden, cot_full, (((0,), (0,)), ((), ())), preferred_element_type=jnp.float32
     )

time: 724 us -> 699 us (0.965)
  waiting for transfers between devices: 348 us -> 315 us
    all_gather x1 -> x0, waiting for transfers between devices: 27.2 us -> none  [shards(): cot_full = lax.all_gather(cotangent, 'seq', axis=1, tiled=True)]
    ppermute x0 -> x3, waiting for transfers between devices: none -> 27.1 us  [the longest x2 27.1 us: gather_around(): from_left = lax.ppermute(from_left, axis, upward)]
    all_gather x1, waiting for transfers between devices: 22.6 us -> 0.01 us  [shards(): whole_rows = lax.all_gather(local_rows, 'seq', axis=1, tiled=True)]
    unnamed x11 -> x10, waiting for transfers between devices: 97.9 us -> 96.5 us
  transfers between devices with their start and end apart: 11 -> 13, of which waited for: 8 -> 8; matrix products, arithmetic and copies ran while one was open for 7% -> 7% of each run, Pallas kernels for 0% -> 0%
where the time goes in v1:
time: 699 us; the launch traced here: 698 us
  waiting for transfers between devices  315 us (45%)
  blocking collectives  252 us (36%)
  local copies, waits for them, and re-layouts  40.3 us (6%)
  starting transfers between devices  30.5 us (4%)
  matrix products  22.8 us (3%)
  other arithmetic  22.1 us (3%)
  between operations  15.8 us (2%)
    psum x1, blocking collectives, shards(): gain_sum, kernel_sum = lax.psum((gain_term, kernel_term), 'dp')  252 us
    unnamed x10, waiting for transfers between devices  96.5 us
    all_gather x1, waiting for transfers between devices, shards(): lax.all_gather(expand, 'dp', axis=0, tiled=True).reshape(D, 2 * quarter)  75.8 us
    all_gather x1, waiting for transfers between devices, shards(): project_full = lax.all_gather(project, 'dp', axis=1, tiled=True)  69.2 us
    psum x1, waiting for transfers between devices, shards(): lax.psum(scaled_part.astype(jnp.bfloat16), 'seq').astype(jnp.float32)  29 us
    ppermute x2, waiting for transfers between devices, gather_around(): from_left = lax.ppermute(from_left, axis, upward)  27.1 us
  transfers between devices with their start and end apart: 13, of which 8 were waited for; matrix products, arithmetic and copies ran while one was open for 7% of the time, Pallas kernels for 0%

profile of v1, /device:TPU:4, one launch (start us, length us, event | category | flops | bytes accessed | tf_op | source)
XLA Modules:
  0.0 698.3 jit_solution(10989659867946944871)
XLA Ops:
  7.2 0.7 fusion.22
  8.6 1.2 reduce-window.6
  10.2 0.7 compare_select_fusion.3
  10.9 2.4 scatter_custom_fusion
  14.1 2.3 gather_fusion.1
  17.1 12.1 %all-to-all-start.1 = ((s32[64,1,8]{2,1,0:T(1,128)}), s32[64,1,8]{2,1,0:T(1,128)S(1)}, u32[]{:S(2)}, u32[]{:S(2)}) async-start(s32[64,1,8]{2,1,0:T(1,128)} %bitcast.4), calls=%async_computation.1 | async-start | bytes 65536 | tf_op jit(solution)/shard_map/all_to_all | solution.py:108
  29.3 2.6 gather_fusion
  31.9 6.8 all-to-all-done.1
  38.7 4.6 all-to-all-start
  43.9 0.7 reduce.23
  44.8 2.4 scatter_custom_fusion.1
  47.2 10.6 %all-to-all-done = bf16[64,8,384]{2,1,0:T(8,128)(2,1)S(1)} async-done(((bf16[64,8,384]{2,1,0:T(8,128)(2,1)}), bf16[64,8,384]{2,1,0:T(8,128)(2,1)S(1)}, u32[]{:S(2)}, u32[]{:S(2)}) %all-to-all-start) | async-done | bytes 393248 | tf_op jit(solution)/shard_map/all_to_all | solution.py:107
  57.9 2.6 gather_fusion.2
  61.3 1.3 collective-permute-start
  62.6 0.8 collective-permute-start.1
  65.0 9.2 %collective-permute-done = bf16[512,384]{1,0:T(8,128)(2,1)S(1)} collective-permute-done((bf16[512,384]{1,0:T(8,128)(2,1)S(1)}, bf16[512,384]{1,0:T(8,128)(2,1)S(1)}, u32[]{:S(2)}, u32[]{:S(2)}) %collective-permute-start) | collective-permute-done | bytes 393248 | tf_op jit(solution)/shard_map/ppermute | solution.py:21
  75.5 17.9 %collective-permute-done.2 = bf16[512,384]{1,0:T(8,128)(2,1)S(1)} collective-permute-done((bf16[512,384]{1,0:T(8,128)(2,1)S(1)}, bf16[512,384]{1,0:T(8,128)(2,1)S(1)}, u32[]{:S(2)}, u32[]{:S(2)}) %collective-permute-start.2) | collective-permute-done | bytes 393248 | tf_op jit(solution)/shard_map/ppermute | solution.py:21
  93.6 1.2 copy-done.6
  94.7 1.8 convert_reduce_fusion
  97.7 75.8 %all-gather.5.cloned.1.call-done = bf16[1536,2,384]{2,1,0:T(2,128)(2,1)} async-done(((bf16[24,2,384]{2,1,0:T(2,128)(2,1)}), bf16[1536,2,384]{2,1,0:T(2,128)(2,1)}) %all-gather.5.cloned.1.call-update) | async-done | bytes 2359312 | tf_op jit(solution)/shard_map/all_gather | solution.py:119
  173.5 2.2 copy.23
  175.7 2.2 fusion.13
  178.3 0.9 copy-done.3
  179.3 2.0 multiply_add_fusion
  181.4 69.2 %all-gather.7.cloned.1.call-done = bf16[384,1536]{0,1:T(8,128)(2,1)} async-done(((bf16[384,24]{0,1:T(8,128)(2,1)}), bf16[384,1536]{0,1:T(8,128)(2,1)}) %all-gather.7.cloned.1.call-update) | async-done | bytes 1179664 | tf_op jit(solution)/shard_map/all_gather | solution.py:120
  250.7 7.9 %multiply_reduce_fusion.1 = (f32[384]{0:T(512)}, f32[384]{0:T(512)}, f32[384]{0:T(512)}, f32[384]{0:T(512)}, f32[384]{0:T(512)}, /*index=5*/f32[384]{0:T(512)}, ...) fusion(f32[512,384]{1,0:T(8,128)} %copy-done.3, ...), kind=kOutput, calls=%fused_computation.36 | convolution fusion | flops 611054208 | bytes 5932032 | tf_op jit(solution)/shard_map/dot_general | solution.py:141
  258.7 0.7 multiply_multiply_fusion.7
  261.2 0.9 copy-done.5
  262.2 2.6 convolution_convert_fusion
  264.9 0.9 copy-done.10
  265.9 3.8 fusion.12
  269.6 8.2 %copy.19 = f32[1536,2,384]{2,1,0:T(2,128)} copy(f32[1536,2,384]{0,2,1:T(8,128)} %bitcast.41) | data formatting | bytes 9437184 | tf_op jit(solution)/shard_map/reshape | solution.py:156
  277.9 2.6 convolution_convert_fusion.1
  280.6 1.6 copy.20
  282.5 1.1 copy-done.7
  283.6 3.6 fusion.46
  287.9 29.0 %all-reduce.21.cloned.1.call-done = bf16[512,1536]{1,0:T(8,128)(2,1)} async-done(((bf16[512,1536]{1,0:T(8,128)(2,1)}), bf16[512,1536]{1,0:T(8,128)(2,1)}) %all-reduce.21.cloned.1.call-update) | async-done | bytes 1572880 | tf_op jit(solution)/shard_map/psum | solution.py:167
  317.0 1.9 convert_element_type.110
  318.9 1.1 fusion.11
  320.5 2.6 gather_fusion.3
  323.1 10.5 %all-to-all-start.2 = ((bf16[64,8,384]{2,1,0:T(8,128)(2,1)}), bf16[64,8,384]{2,1,0:T(8,128)(2,1)S(1)}, u32[]{:S(2)}, u32[]{:S(2)}) async-start(bf16[64,8,384]{2,1,0:T(8,128)(2,1)} %bitcast.7), calls=%async_computation.2 | async-start | bytes 786432 | tf_op jit(solution)/shard_map/all_to_all | solution.py:179
  335.1 251.8 %all-reduce.17 = (f32[384]{0:T(512)S(1)}, f32[9,384]{1,0:T(8,128)S(1)}) all-reduce(f32[384]{0:T(512)S(1)} %get-tuple-element.30, f32[9,384]{1,0:T(8,128)S(1)} %stack.39), channel_id=1, replica_groups=mesh['dp'=64,'seq'=4] {'dp'}, use_global_device_ids=true, to_apply=%region_12.13 | all-reduce | flops 3840 | bytes 30720 | tf_op jit(solution)/shard_map/psum | solution.py:175
  588.1 2.6 gather_fusion.4
  590.7 1.6 dynamic-slice_multiply_fusion
  592.3 1.2 copy.21
  593.5 0.8 add_convert_fusion
  594.3 95.7 %reduce-scatter.9.cloned.1.call-done = f32[384,24]{0,1:T(8,128)} async-done(((f32[384,1536]{0,1:T(8,128)}), f32[384,24]{0,1:T(8,128)}) %reduce-scatter.9.cloned.1.call-update) | async-done | bytes 36880
  690.0 1.4 broadcast_multiply_fusion.2
  (189 shorter events, 14.0 us)
Async XLA Ops:
  7.2 22.1 %copy-start.11 = (bf16[512,384]{1,0:T(8,128)(2,1)S(1)}, bf16[512,384]{1,0:T(8,128)(2,1)}, u32[]{:S(2)}) copy-start(bf16[512,384]{1,0:T(8,128)(2,1)} %param.8) | copy-start | bytes 1179652
  10.9 3.2 copy-start.44
  17.1 21.6 %all-to-all-start.1 = ((s32[64,1,8]{2,1,0:T(1,128)}), s32[64,1,8]{2,1,0:T(1,128)S(1)}, u32[]{:S(2)}, u32[]{:S(2)}) async-start(s32[64,1,8]{2,1,0:T(1,128)} %bitcast.4), calls=%async_computation.1 | async-start | bytes 65536 | tf_op jit(solution)/shard_map/all_to_all | solution.py:108
  38.7 19.1 %all-to-all-start = ((bf16[64,8,384]{2,1,0:T(8,128)(2,1)}), bf16[64,8,384]{2,1,0:T(8,128)(2,1)S(1)}, u32[]{:S(2)}, u32[]{:S(2)}) async-start(bf16[64,8,384]{2,1,0:T(8,128)(2,1)} %bitcast.2), calls=%async_computation | async-start | bytes 786432 | tf_op jit(solution)/shard_map/all_to_all | solution.py:107
  43.3 51.4 %all-gather.9.cloned.1.call-start = ((), (), s32[]{:S(2)}) async-start(), calls=%async_computation.8 | async-start | bytes 1966080 | tf_op jit(solution)/shard_map/all_gather | solution.py:111
  44.7 13.1 %copy-start.46 = (s32[512,1]{0,1:T(1,128)}, s32[512,1]{0,1:T(1,128)S(1)}, u32[]{:S(2)}) copy-start(s32[512,1]{0,1:T(1,128)S(1)} %compare_select_fusion) | copy-start | bytes 6148
  57.9 3.4 copy-start.8
  60.5 3.2 copy-start.49
  60.5 3.9 copy-start.48
  60.5 113.0 %all-gather.5.cloned.1.call-start = ((), (), s32[]{:S(2)}) async-start(), calls=%async_computation.5 | async-start | bytes 2396160 | tf_op jit(solution)/shard_map/all_gather | solution.py:119
  61.2 189.3 %all-gather.7.cloned.1.call-start = ((), (), s32[]{:S(2)}) async-start(), calls=%async_computation.6 | async-start | bytes 1198080 | tf_op jit(solution)/shard_map/all_gather | solution.py:120
  61.3 12.8 %collective-permute-start = (bf16[512,384]{1,0:T(8,128)(2,1)S(1)}, bf16[512,384]{1,0:T(8,128)(2,1)S(1)}, u32[]{:S(2)}, u32[]{:S(2)}) collective-permute-start(bf16[512,384]{1,0:T(8,128)(2,1)S(1)} %copy-done.8), channel_id=1, source_target_pairs={{0,1},{1,2},{2,3},{3,0},{4,5},{5,6},{6,7},{7,4},{8,9},{9,10},{10,1... | collective-permute-start | bytes 1179656 | tf_op jit(solution)/shard_map/ppermute | solution.py:21
  62.6 12.9 %collective-permute-start.1 = (bf16[512,384]{1,0:T(8,128)(2,1)S(1)}, bf16[512,384]{1,0:T(8,128)(2,1)S(1)}, u32[]{:S(2)}, u32[]{:S(2)}) collective-permute-start(bf16[512,384]{1,0:T(8,128)(2,1)S(1)} %copy-done.8), channel_id=1, source_target_pairs={{0,3},{1,0},{2,1},{3,2},{4,7},{5,4},{6,5},{7,6},{8,11},{9,8},{10,9... | collective-permute-start | bytes 1179656 | tf_op jit(solution)/shard_map/ppermute | solution.py:26
  63.4 253.5 %all-reduce.21.cloned.1.call-start = ((), (), s32[]{:S(2)}) async-start(), calls=%async_computation.7 | async-start | bytes 3145728 | tf_op jit(solution)/shard_map/psum | solution.py:167
  74.1 19.3 %collective-permute-start.2 = (bf16[512,384]{1,0:T(8,128)(2,1)S(1)}, bf16[512,384]{1,0:T(8,128)(2,1)S(1)}, u32[]{:S(2)}, u32[]{:S(2)}) collective-permute-start(bf16[512,384]{1,0:T(8,128)(2,1)S(1)} %collective-permute-done), channel_id=1, source_target_pairs={{0,1},{1,2},{2,3},{3,0},{4,5},{5,6},{6,7},{7,4},{8,9},{9,10},{10,1... | collective-permute-start | bytes 1179656 | tf_op jit(solution)/shard_map/ppermute | solution.py:21
  96.6 79.1 %copy-start.36 = (f32[512]{0:T(512)}, f32[512]{0:T(512)S(1)}, u32[]{:S(2)}) copy-start(f32[512]{0:T(512)S(1)} %broadcast_multiply_fusion.7) | copy-start | bytes 6148
  173.5 2.2 copy-start.38
  173.5 2.2 copy-start.40
  175.7 2.3 copy-start.4
  250.6 8.0 %copy-start.15 = (f32[512]{0:T(512)S(1)}, f32[512]{0:T(512)}, u32[]{:S(2)}) copy-start(f32[512]{0:T(512)} %get-tuple-element.47) | copy-start | bytes 6148
  250.6 8.0 %copy-start.17 = (f32[512]{0:T(512)S(1)}, f32[512]{0:T(512)}, u32[]{:S(2)}) copy-start(f32[512]{0:T(512)} %get-tuple-element.48) | copy-start | bytes 6148
  250.6 8.0 %copy-start.19 = (f32[512]{0:T(512)S(1)}, f32[512]{0:T(512)}, u32[]{:S(2)}) copy-start(f32[512]{0:T(512)} %get-tuple-element.49) | copy-start | bytes 6148
  250.6 8.0 %copy-start.21 = (f32[384]{0:T(512)S(1)}, f32[384]{0:T(512)}, u32[]{:S(2)}) copy-start(f32[384]{0:T(512)} %get-tuple-element.17) | copy-start | bytes 4612
  250.6 8.0 %copy-start.23 = (f32[384]{0:T(512)S(1)}, f32[384]{0:T(512)}, u32[]{:S(2)}) copy-start(f32[384]{0:T(512)} %get-tuple-element.18) | copy-start | bytes 4612
  250.6 8.0 %copy-start.25 = (f32[384]{0:T(512)S(1)}, f32[384]{0:T(512)}, u32[]{:S(2)}) copy-start(f32[384]{0:T(512)} %get-tuple-element.19) | copy-start | bytes 4612
  250.6 8.0 %copy-start.27 = (f32[384]{0:T(512)S(1)}, f32[384]{0:T(512)}, u32[]{:S(2)}) copy-start(f32[384]{0:T(512)} %get-tuple-element.20) | copy-start | bytes 4612
  250.6 8.0 %copy-start.29 = (f32[384]{0:T(512)S(1)}, f32[384]{0:T(512)}, u32[]{:S(2)}) copy-start(f32[384]{0:T(512)} %get-tuple-element.21) | copy-start | bytes 4612
  250.6 8.0 %copy-start.31 = (f32[384]{0:T(512)S(1)}, f32[384]{0:T(512)}, u32[]{:S(2)}) copy-start(f32[384]{0:T(512)} %get-tuple-element.22) | copy-start | bytes 4612
  250.6 8.0 %copy-start.33 = (f32[384]{0:T(512)S(1)}, f32[384]{0:T(512)}, u32[]{:S(2)}) copy-start(f32[384]{0:T(512)} %get-tuple-element.23) | copy-start | bytes 4612
  250.6 8.0 %copy-start.35 = (f32[384]{0:T(512)S(1)}, f32[384]{0:T(512)}, u32[]{:S(2)}) copy-start(f32[384]{0:T(512)} %get-tuple-element.25) | copy-start | bytes 4612
  260.2 1.9 copy-start.5
  264.8 325.9 %all-reduce.23.cloned.1.call-start = ((), (), s32[]{:S(2)}) async-start(), calls=%async_computation.10 | async-start | bytes 9437184
  277.9 314.4 %reduce-scatter.7.cloned.1.call-start = ((), (), s32[]{:S(2)}) async-start(), calls=%async_computation.9 | async-start | bytes 1966080
  282.2 407.8 %reduce-scatter.9.cloned.1.call-start = ((), (), s32[]{:S(2)}) async-start(), calls=%async_computation.11 | async-start | bytes 2396160
  317.0 1.9 copy-start.1
  320.4 13.2 %copy-start.59 = (u32[256]{0:T(256)S(1)}, u32[256]{0:T(256)}, u32[]{:S(2)}) copy-start(u32[256]{0:T(256)} %constant.136) | copy-start | bytes 3076
  320.4 14.4 %copy-start.45 = (s32[512]{0:T(512)S(1)}, s32[512]{0:T(512)}, u32[]{:S(2)}) copy-start(s32[512]{0:T(512)} %copy-done.44) | copy-start | bytes 6148
  320.4 14.4 %copy-start.58 = (f32[384]{0:T(512)S(1)}, f32[384]{0:T(512)}, u32[]{:S(2)}) copy-start(f32[384]{0:T(512)} %get-tuple-element.9) | copy-start | bytes 4612
  320.4 14.4 %copy-start.57 = (f32[384]{0:T(512)S(1)}, f32[384]{0:T(512)}, u32[]{:S(2)}) copy-start(f32[384]{0:T(512)} %get-tuple-element.10) | copy-start | bytes 4612
  320.4 14.4 %copy-start.56 = (f32[384]{0:T(512)S(1)}, f32[384]{0:T(512)}, u32[]{:S(2)}) copy-start(f32[384]{0:T(512)} %get-tuple-element.11) | copy-start | bytes 4612
  320.4 14.5 %copy-start.55 = (f32[384]{0:T(512)S(1)}, f32[384]{0:T(512)}, u32[]{:S(2)}) copy-start(f32[384]{0:T(512)} %get-tuple-element.12) | copy-start | bytes 4612
  320.5 14.5 %copy-start.54 = (f32[384]{0:T(512)S(1)}, f32[384]{0:T(512)}, u32[]{:S(2)}) copy-start(f32[384]{0:T(512)} %get-tuple-element.16) | copy-start | bytes 4612
  320.5 14.5 %copy-start.53 = (f32[384]{0:T(512)S(1)}, f32[384]{0:T(512)}, u32[]{:S(2)}) copy-start(f32[384]{0:T(512)} %get-tuple-element.13) | copy-start | bytes 4612
  320.5 14.5 %copy-start.52 = (f32[384]{0:T(512)S(1)}, f32[384]{0:T(512)}, u32[]{:S(2)}) copy-start(f32[384]{0:T(512)} %get-tuple-element.14) | copy-start | bytes 4612
  320.5 14.5 %copy-start.51 = (f32[384]{0:T(512)S(1)}, f32[384]{0:T(512)}, u32[]{:S(2)}) copy-start(f32[384]{0:T(512)} %get-tuple-element.15) | copy-start | bytes 4612
  320.5 14.5 %copy-start.50 = (f32[384]{0:T(512)S(1)}, f32[384]{0:T(512)}, u32[]{:S(2)}) copy-start(f32[384]{0:T(512)} %get-tuple-element.8) | copy-start | bytes 4612
  323.1 265.0 %all-to-all-start.2 = ((bf16[64,8,384]{2,1,0:T(8,128)(2,1)}), bf16[64,8,384]{2,1,0:T(8,128)(2,1)S(1)}, u32[]{:S(2)}, u32[]{:S(2)}) async-start(bf16[64,8,384]{2,1,0:T(8,128)(2,1)} %bitcast.7), calls=%async_computation.2 | async-start | bytes 786432 | tf_op jit(solution)/shard_map/all_to_all | solution.py:179
  588.1 5.4 copy-start.2
  (25 other events, 29.0 us)
Sparse Core Ops, SparseCore 0:
  60.6 33.2 all-gather.8
  96.6 76.8 all-gather.4
  176.2 74.3 all-gather.6
  264.9 51.9 all-reduce.20
  320.4 201.8 all-reduce.22
  524.7 25.3 reduce-scatter.6
  554.2 135.7 reduce-scatter.8
